TPU v7x, 128 devices: a whole 4x4x4 slice. The times are simulated.
128 devices in a mesh: redist: 32 (over x, y, core), rep: 4 (over z).
Axes of the slice: x: 4, y: 4, z: 4, core: 2. Of those that a mesh axis runs over, the one named last changes fastest.
Arguments:
- amplitudes: bfloat16 [4, 128, 1024, 1024], P(None, ('redist', 'rep')), may hold values from -6 to 6
- integrals: bfloat16 [128, 1024, 2, 1024], P(None, 'redist'), may hold values from -0.046875 to 0.046875
- occ_irrep: int32 [128], replicated, may hold values from 0 to 7, as said below
- virt_irrep: int32 [1024], replicated, may hold values from 0 to 7, as said below
Outputs:
- cycle_term: float32 [4, 1024, 2, 1024], P(None, None, None, 'redist')
Inputs may be any that keep to these rules, and one draw needn't show every extreme that they name: `occ_irrep`: labels never fall along the orbitals; each of the 8 irreps holds one contiguous range of between n // 16 and 3 * n // 16 orbitals, n being 128 or 1024. `virt_irrep`: labels never fall along the orbitals; each of the 8 irreps holds one contiguous range of between n // 16 and 3 * n // 16 orbitals, n being 128 or 1024.
All inputs are finite; a program needn't handle non-finite values.
Results may differ from a plain program's by a relative error of at most 0.0003.
Values may be sent and summed in bfloat16 or wider, within the bound.
No kernel may reach another device: no remote copies, remote signals or barrier semaphores. Data moves between devices by JAX's collectives and lax.ppermute only.
A program may use at most 192 MiB of HBM per device.

v0:
```python
import jax
import jax.numpy as jnp
from jax import lax
from jax.sharding import PartitionSpec as P


def over_pieces(shard, axis):
    return lax.all_gather(shard, axis).sum(0)


def irrep_allowed(occ_rows, occ_cols, virt_rows, virt_cols):
    pair_ik = jnp.bitwise_xor(occ_rows[:, None], occ_cols[None, :])
    pair_ac = jnp.bitwise_xor(virt_rows[:, None], virt_cols[None, :])
    return pair_ik[:, :, None, None] == pair_ac[None, None, :, :]


def integral_allowed(occ_ks, virt_cs, occ_js, virt_bs):
    pair_kc = jnp.bitwise_xor(occ_ks[:, None], virt_cs[None, :])
    pair_jb = jnp.bitwise_xor(occ_js[:, None], virt_bs[None, :])
    return pair_kc[:, :, None, None] == pair_jb[None, None, :, :]


def contract(masked, operand):
    return lax.dot_general(
        masked, operand, (((1, 3), (0, 1)), ((), ())), preferred_element_type=jnp.float32
    )


def body(amplitudes, integrals, occ_irrep, virt_irrep):
    n_redist = lax.axis_size("redist")
    n_rep = lax.axis_size("rep")
    dev_index = lax.axis_index("redist")
    rep_index = lax.axis_index("rep")
    i_slab, k_block, v_width, _ = amplitudes.shape
    c_block = integrals.shape[1]
    j_slab = integrals.shape[2]
    occ_rows = occ_irrep[:i_slab]
    occ_js = occ_irrep[:j_slab]
    zero_value = jnp.zeros((), amplitudes.dtype)
    grouped_ints = integrals.reshape(n_redist, n_rep, k_block, c_block, j_slab, v_width)
    ints_mine = lax.dynamic_slice_in_dim(grouped_ints, rep_index, 1, 1).reshape(
        n_redist * k_block, c_block, j_slab, v_width
    )
    moved = lax.all_to_all(ints_mine, "redist", split_axis=0, concat_axis=1, tiled=True)
    occ_cols = lax.dynamic_slice_in_dim(
        occ_irrep, (dev_index * n_rep + rep_index) * k_block, k_block
    )
    masked = jnp.where(
        irrep_allowed(occ_rows, occ_cols, virt_irrep, virt_irrep), amplitudes, zero_value
    )
    sym_ints = jnp.where(
        integral_allowed(occ_cols, virt_irrep, occ_js, virt_irrep), moved, zero_value
    )
    partial_value = contract(masked, sym_ints)
    shares = lax.psum_scatter(partial_value, "redist", scatter_dimension=3, tiled=True)
    return over_pieces(shares, "rep")


def solution(mesh):
    placed = (P(None, ("redist", "rep"), None, None), P(None, "redist", None, None), P(), P())
    return jax.shard_map(
        body, mesh=mesh, in_specs=placed, out_specs=P(None, None, None, "redist"), check_vma=False
    )
```

profile of v0, /device:TPU:6, one launch (start us, length us, event | category | flops | bytes accessed | tf_op | source)
XLA Modules:
  0.0 345.1 jit_solution(3370255375633369557)
XLA Ops:
  6.5 16.4 %copy.8 = bf16[128,32,2,1024]{3,1,2,0:T(8,128)(2,1)} copy(bf16[128,32,2,1024]{3,2,1,0:T(2,128)(2,1)} %param.5) | data formatting | bytes 33554432 | tf_op args[1]
  23.0 4.9 %dynamic-slice_bitcast_fusion = bf16[32,32,2,1024]{3,1,2,0:T(8,128)(2,1)} fusion(bf16[32,4,1,32,2,1024]{5,3,4,2,1,0:T(8,128)(2,1)} %bitcast.16, s32[]{:T(128)S(6)} %select_n.23), kind=kLoop, calls=%fused_computation.6 | loop fusion | bytes 8388612 | tf_op jit(solution)/shard_map/reshape | solution.py:41
  27.9 0.0 copy-start.1
  27.9 0.0 copy-start
  27.9 7.8 %all-to-all-start = ((bf16[32,32,2,1024]{3,1,2,0:T(8,128)(2,1)}), bf16[32,32,2,1024]{3,1,2,0:T(8,128)(2,1)}, u32[]{:S(2)}, u32[]{:S(2)}) async-start(bf16[32,32,2,1024]{3,1,2,0:T(8,128)(2,1)} %dynamic-slice_bitcast_fusion), calls=%async_computation | async-start | bytes 8388608 | tf_op jit(solution)/shard_map/all_to_all | solution.py:44
  35.7 0.0 reduce-scatter.2.cloned.1.call-start
  35.8 0.0 copy-done.1
  35.8 0.6 dynamic_slice.6
  36.4 0.0 copy-done
  36.4 0.6 broadcast_xor_fusion.2
  37.0 0.1 eq.44
  37.1 0.6 slice_xor_fusion
  37.7 0.1 broadcast_xor_fusion.1
  37.8 2.4 broadcast_xor_fusion
  40.2 46.2 %all-to-all-done = bf16[32,32,2,1024]{3,1,2,0:T(8,128)(2,1)} async-done(((bf16[32,32,2,1024]{3,1,2,0:T(8,128)(2,1)}), bf16[32,32,2,1024]{3,1,2,0:T(8,128)(2,1)}, u32[]{:S(2)}, u32[]{:S(2)}) %all-to-all-start) | async-done | bytes 4194336 | tf_op jit(solution)/shard_map/all_to_all | solution.py:44
  86.5 2.8 compare_select_fusion.1
  89.3 2.4 copy.9
  91.7 25.1 %fusion.1 = f32[4,1024,2,1024]{1,3,2,0:T(8,128)} fusion(bf16[1024,2,1024,1]{2,0,1,3:T(8,128)(2,1)} %bitcast.18, bf16[4,1,1024,1024]{3,2,1,0:T(8,128)(2,1)} %param.4, s32[1024,1024]{1,0:T(8,128)} %broadcast_xor_fusion, s32[4]{0:T(128)S(1)} %slice_xor_fusion), kind=kOutput, calls=%fused_computation.2 | convolution fusion | flops 17188257792 | bytes 50331664 | tf_op jit(solution)/shard_map/dot_general | solution.py:24
  116.7 0.0 reduce-scatter.2.cloned.1.call-update
  116.8 0.0 all-gather.3.cloned.1.call-start
  116.8 168.0 %reduce-scatter.2.cloned.1.call-done = f32[4,1024,2,32]{1,3,2,0:T(8,128)} async-done(((f32[4,1024,2,1024]{1,3,2,0:T(8,128)}), f32[4,1024,2,32]{1,3,2,0:T(8,128)}) %reduce-scatter.2.cloned.1.call-update) | async-done | bytes 1048592 | tf_op jit(solution)/shard_map/reduce_scatter | solution.py:55
  284.8 0.0 all-gather.3.cloned.1.call-update
  284.8 49.8 %all-gather.3.cloned.1.call-done = f32[16,1024,2,32]{1,3,2,0:T(8,128)} async-done(((f32[4,1024,2,32]{1,3,2,0:T(8,128)}), f32[16,1024,2,32]{1,3,2,0:T(8,128)}) %all-gather.3.cloned.1.call-update) | async-done | bytes 4194320 | tf_op jit(solution)/shard_map/all_gather | solution.py:8
  334.6 3.7 %reduce_sum.9 = f32[4,1024,2,32]{1,3,2,0:T(8,128)} reduce(f32[4,4,1024,2,32]{2,4,3,1,0:T(8,128)} %bitcast.17, f32[]{:T(128)} %constant.18.clone.1), dimensions={0}, to_apply=%region_1.2 | reduce | flops 786432 | bytes 5242884 | tf_op jit(solution)/shard_map/reduce_sum | solution.py:8
Async XLA Ops:
  27.9 7.9 %copy-start.1 = (s32[128]{0:T(128)S(1)}, s32[128]{0:T(128)}, u32[]{:S(2)}) copy-start(s32[128]{0:T(128)} %param.6) | copy-start | bytes 1540
  27.9 8.5 %copy-start = (s32[1024]{0:T(1024)S(1)}, s32[1024]{0:T(1024)}, u32[]{:S(2)}) copy-start(s32[1024]{0:T(1024)} %param.7) | copy-start | bytes 12292
  27.9 58.6 %all-to-all-start = ((bf16[32,32,2,1024]{3,1,2,0:T(8,128)(2,1)}), bf16[32,32,2,1024]{3,1,2,0:T(8,128)(2,1)}, u32[]{:S(2)}, u32[]{:S(2)}) async-start(bf16[32,32,2,1024]{3,1,2,0:T(8,128)(2,1)} %dynamic-slice_bitcast_fusion), calls=%async_computation | async-start | bytes 8388608 | tf_op jit(solution)/shard_map/all_to_all | solution.py:44
  35.7 249.1 %reduce-scatter.2.cloned.1.call-start = ((), (), s32[]{:S(2)}) async-start(), calls=%async_computation.2 | async-start | bytes 34603008 | tf_op jit(solution)/shard_map/reduce_scatter | solution.py:55
  116.8 217.8 %all-gather.3.cloned.1.call-start = ((), (), s32[]{:S(2)}) async-start(), calls=%async_computation.3 | async-start | bytes 5242880 | tf_op jit(solution)/shard_map/all_gather | solution.py:8
Sparse Core Ops, SparseCore 0:
  116.9 167.8 reduce-scatter.1
  286.5 48.1 all-gather.2
where the time goes:
time: 346 us; the launch traced here: 345 us
  waiting for transfers between devices  264 us (76%)
  matrix products  25.1 us (7%)
  local copies, waits for them, and re-layouts  24.4 us (7%)
  between operations  13.5 us (4%)
  other arithmetic  10.3 us (3%)
  starting transfers between devices  7.88 us (2%)
    reduce_scatter x1, waiting for transfers between devices, body(): lax.psum_scatter(partial_value, 'redist', scatter_dimension=3, tiled=True)  168 us
    all_gather x1, waiting for transfers between devices, over_pieces(): return lax.all_gather(shard, axis).sum(0)  49.8 us
    all_to_all x1, waiting for transfers between devices, body(): lax.all_to_all(ints_mine, 'redist', split_axis=0, concat_axis=1, tiled=True)  46.2 us
    dot_general x1, matrix products, contract(): lax.dot_general(masked, operand, (((1, 3), (0, 1)), ((), ())), preferred_...  25.1 us
    unnamed x5, local copies, waits for them, and re-layouts  16.4 us
    all_to_all x1, starting transfers between devices, body(): lax.all_to_all(ints_mine, 'redist', split_axis=0, concat_axis=1, tiled=True)  7.79 us
  transfers between devices with their start and end apart: 3, of which 3 were waited for; matrix products, arithmetic and copies ran while one was open for 1% of the time, Pallas kernels for 0%

commit v1 on v0

v1 whole, which is shorter than its diff:
```python
import jax
import jax.numpy as jnp
from jax import lax
from jax.sharding import PartitionSpec as P

N_IRREPS = 8


def irrep_windows(virt_irrep, width):
    count = virt_irrep.shape[0]
    starts = jnp.sum(
        (virt_irrep[None, :] < jnp.arange(N_IRREPS, dtype=virt_irrep.dtype)[:, None]).astype(jnp.int32),
        axis=1,
    )
    return jnp.minimum(starts, count - width)


def parts_in(span, count):
    return min(N_IRREPS, -(-span // (count // 16)) + 1)


def body(amplitudes, integrals, occ_irrep, virt_irrep):
    n_redist = lax.axis_size("redist")
    n_rep = lax.axis_size("rep")
    dev_index = lax.axis_index("redist")
    rep_index = lax.axis_index("rep")
    i_slab, k_block, v_width, _ = amplitudes.shape
    c_block = integrals.shape[1]
    j_slab = integrals.shape[2]
    width = 3 * v_width // 16
    wins = irrep_windows(virt_irrep, width)
    occ_rows = occ_irrep[:i_slab]
    occ_js = occ_irrep[:j_slab]

    grouped = integrals.reshape(n_redist, n_rep, k_block, c_block, j_slab, v_width)
    mine = lax.dynamic_index_in_dim(grouped, rep_index, 1, keepdims=False)
    mine = mine.reshape(n_redist * k_block, c_block, j_slab, v_width)
    dest_k = (
        (jnp.arange(n_redist, dtype=jnp.int32)[:, None] * n_rep + rep_index) * k_block
        + jnp.arange(k_block, dtype=jnp.int32)[None, :]
    ).reshape(-1)
    dest_lab = occ_irrep[dest_k]
    c_lab = lax.dynamic_slice_in_dim(virt_irrep, dev_index * c_block, c_block)
    n_cparts = parts_in(c_block, v_width)
    pieces = []
    for d in range(n_redist * k_block):
        row = mine[d]
        piece = jnp.zeros((c_block, j_slab, width), integrals.dtype)
        for p in range(n_cparts):
            lab = jnp.minimum(c_lab[0] + p, N_IRREPS - 1)
            start = wins[jnp.bitwise_xor(lab, dest_lab[d])]
            cut = lax.dynamic_slice_in_dim(row, start, width, axis=2)
            piece = jnp.where((c_lab == c_lab[0] + p)[:, None, None], cut, piece)
        pieces.append(piece)
    packed = jnp.stack(pieces)
    moved = lax.all_to_all(packed, "redist", split_axis=0, concat_axis=1, tiled=True)
    moved = moved.reshape(k_block, n_redist * c_block, j_slab, width)

    my_k0 = (dev_index * n_rep + rep_index) * k_block
    blocks = []
    for kk in range(k_block):
        k_lab = occ_irrep[my_k0 + kk]
        amp = amplitudes[:, kk]
        ints = moved[kk]
        pair_ik = jnp.bitwise_xor(occ_rows, k_lab)
        per_g = []
        for g in range(N_IRREPS):
            c_irrep = jnp.bitwise_xor(g, k_lab)
            wa = wins[g]
            wc = wins[c_irrep]
            a_lab = lax.dynamic_slice_in_dim(virt_irrep, wa, width)
            cw_lab = lax.dynamic_slice_in_dim(virt_irrep, wc, width)
            a_blk = lax.dynamic_slice(amp, (0, wa, wc), (i_slab, width, width))
            allowed = pair_ik[:, None, None] == jnp.bitwise_xor(a_lab[:, None], cw_lab[None, :])[None]
            a_blk = jnp.where(allowed, a_blk, jnp.zeros((), a_blk.dtype))
            i_blk = lax.dynamic_slice_in_dim(ints, wc, width, axis=0)
            sym = (cw_lab == c_irrep)[:, None, None] & (
                jnp.bitwise_xor(cw_lab, k_lab)[:, None, None]
                == jnp.bitwise_xor(occ_js[:, None], a_lab[None, :])[None]
            )
            i_blk = jnp.where(sym, i_blk, jnp.zeros((), i_blk.dtype))
            blk = lax.dot_general(
                i_blk, a_blk, (((0,), (2,)), ((), ())), preferred_element_type=jnp.float32
            )
            per_g.append(jnp.transpose(blk, (1, 0, 2, 3)).reshape(width, -1))
        blocks.append(jnp.concatenate(per_g, axis=0))
    every = blocks[0]
    for more in blocks[1:]:
        every = every + more
    b_pos = jnp.arange(v_width, dtype=jnp.int32)
    pick = virt_irrep * width + (b_pos - wins[virt_irrep])
    compact = jnp.take(every, pick, axis=0)

    shares = lax.psum_scatter(compact, ("redist", "rep"), scatter_dimension=0, tiled=True)
    mine_b = lax.all_gather(shares, "rep", axis=0, tiled=True)

    nb = mine_b.shape[0]
    b_lab = lax.dynamic_slice_in_dim(virt_irrep, dev_index * nb, nb)
    vals = mine_b.reshape(nb, j_slab, i_slab, width).transpose(2, 3, 1, 0)
    out = jnp.zeros((i_slab, v_width, j_slab, nb), jnp.float32)
    for p in range(parts_in(nb, v_width)):
        lab = b_lab[0] + p
        part = jnp.where((b_lab == lab)[None, None, None, :], vals, 0.0)
        start = wins[jnp.minimum(lab, N_IRREPS - 1)]
        placed = lax.dynamic_update_slice(
            jnp.zeros((i_slab, v_width, j_slab, nb), jnp.float32), part, (0, start, 0, 0)
        )
        out = out + placed
    return out


def solution(mesh):
    placed = (P(None, ("redist", "rep"), None, None), P(None, "redist", None, None), P(), P())
    return jax.shard_map(
        body, mesh=mesh, in_specs=placed, out_specs=P(None, None, None, "redist"), check_vma=False
    )
```

time: 346 us -> 605 us (1.75); the launches traced: 345 us -> 597 us
  between operations: 13.5 us -> 215 us
  other arithmetic: 10.3 us -> 69.2 us
  waiting for transfers between devices: 264 us -> 210 us
  local copies, waits for them, and re-layouts: 24.4 us -> 69.4 us
  blocking collectives: 0 us -> 12.3 us
  matrix products: 25.1 us -> 13 us
    all_gather x1 -> x0, waiting for transfers between devices: 49.8 us -> none  [over_pieces(): return lax.all_gather(shard, axis).sum(0)]
    unnamed x0 -> x31, other arithmetic: none -> 48 us
    all_to_all x1, waiting for transfers between devices: 46.2 us -> 0.01 us  [body(): lax.all_to_all(packed, 'redist', split_axis=0, concat_axis=1, tiled=True)]
    reduce_scatter x1, waiting for transfers between devices: 168 us -> 210 us  [body(): lax.psum_scatter(compact, ('redist', 'rep'), scatter_dimension=0, tiled=T...]
    unnamed x5 -> x22, local copies, waits for them, and re-layouts: 16.4 us -> 31.6 us
    gather x0 -> x4, local copies, waits for them, and re-layouts: none -> 14.4 us  [the longest x1 11.4 us: body(): compact = jnp.take(every, pick, axis=0)]
    all_gather x0 -> x1, blocking collectives: none -> 12.3 us  [body(): mine_b = lax.all_gather(shares, 'rep', axis=0, tiled=True)]
    dot_general x1 -> x8, matrix products: 25.1 us -> 13 us  [body(): lax.dot_general(i_blk, a_blk, (((0,), (2,)), ((), ())), preferred_element...]
  transfers between devices with their start and end apart: 3 -> 2, of which waited for: 3 -> 1; matrix products, arithmetic and copies ran while one was open for 1% -> 2% of each run, Pallas kernels for 0% -> 0%
where the time goes in v1:
time: 605 us; the launch traced here: 597 us
  between operations  215 us (36%)
  waiting for transfers between devices  210 us (35%)
  local copies, waits for them, and re-layouts  69.4 us (11%)
  other arithmetic  69.2 us (11%)
  matrix products  13 us (2%)
  blocking collectives  12.3 us (2%)
  starting transfers between devices  8.69 us (1%)
    reduce_scatter x1, waiting for transfers between devices, body(): lax.psum_scatter(compact, ('redist', 'rep'), scatter_dimension=0, tiled=T...  210 us
    unnamed x31, other arithmetic  48 us
    unnamed x22, local copies, waits for them, and re-layouts  31.6 us
    dot_general x8, matrix products, body(): lax.dot_general(i_blk, a_blk, (((0,), (2,)), ((), ())), preferred_element...  13 us
    all_gather x1, blocking collectives, body(): mine_b = lax.all_gather(shares, 'rep', axis=0, tiled=True)  12.3 us
  transfers between devices with their start and end apart: 2, of which 1 were waited for; matrix products, arithmetic and copies ran while one was open for 2% of the time, Pallas kernels for 0%

profile of v1, /device:TPU:6, one launch (start us, length us, event | category | flops | bytes accessed | tf_op | source)
XLA Modules:
  0.0 597.4 jit_solution(7848239957368478515)
XLA Ops:
  6.6 1.4 gather_fusion
  15.3 1.3 dynamic_slice.666
  144.4 16.4 %copy.38 = bf16[128,32,2,1024]{3,1,2,0:T(8,128)(2,1)} copy(bf16[128,32,2,1024]{3,2,1,0:T(2,128)(2,1)} %param.5) | data formatting | bytes 33554432 | tf_op args[1]
  200.8 1.6 constant_dynamic-update-slice_fusion.31
  202.4 1.6 constant_dynamic-update-slice_fusion.30
  204.0 1.6 constant_dynamic-update-slice_fusion.29
  205.5 1.6 constant_dynamic-update-slice_fusion.28
  207.1 1.5 constant_dynamic-update-slice_fusion.27
  208.7 1.5 constant_dynamic-update-slice_fusion.26
  210.2 1.5 constant_dynamic-update-slice_fusion.25
  211.7 1.5 constant_dynamic-update-slice_fusion.24
  213.2 1.5 constant_dynamic-update-slice_fusion.23
  214.8 1.5 constant_dynamic-update-slice_fusion.22
  216.3 1.5 constant_dynamic-update-slice_fusion.21
  217.8 1.5 constant_dynamic-update-slice_fusion.20
  219.3 1.5 constant_dynamic-update-slice_fusion.19
  220.8 1.5 constant_dynamic-update-slice_fusion.18
  222.3 1.5 constant_dynamic-update-slice_fusion.17
  223.9 1.5 constant_dynamic-update-slice_fusion.16
  225.4 1.5 constant_dynamic-update-slice_fusion.15
  227.0 1.6 constant_dynamic-update-slice_fusion.14
  228.6 1.6 constant_dynamic-update-slice_fusion.13
  230.1 1.6 constant_dynamic-update-slice_fusion.12
  231.7 1.6 constant_dynamic-update-slice_fusion.11
  233.3 1.5 constant_dynamic-update-slice_fusion.10
  234.8 1.5 constant_dynamic-update-slice_fusion.9
  236.4 1.5 constant_dynamic-update-slice_fusion.8
  237.9 1.5 constant_dynamic-update-slice_fusion.7
  239.4 1.5 constant_dynamic-update-slice_fusion.6
  241.0 1.5 constant_dynamic-update-slice_fusion.5
  242.5 1.5 constant_dynamic-update-slice_fusion.4
  244.0 1.5 constant_dynamic-update-slice_fusion.3
  245.6 1.6 constant_dynamic-update-slice_fusion.2
  247.2 1.6 constant_dynamic-update-slice_fusion.1
  248.7 1.6 constant_dynamic-update-slice_fusion
  250.3 8.5 %all-to-all-start = ((bf16[32,32,2,192]{3,1,2,0:T(8,128)(2,1)}), bf16[32,32,2,192]{3,1,2,0:T(8,128)(2,1)S(1)}, u32[]{:S(2)}, u32[]{:S(2)}) async-start(bf16[32,32,2,192]{3,1,2,0:T(8,128)(2,1)} %constant_dynamic-update-slice_fusion), calls=%async_computation | async-start | bytes 2097152 | tf_op jit(solution)/shard_map/all_to_all | solution.py:56
  278.9 4.9 compare_and_fusion
  301.0 1.7 fusion.4
  302.6 1.5 copy.41
  304.1 1.6 fusion.1
  305.8 1.5 copy.40
  307.3 2.4 constant_dynamic-update-slice_fusion.39
  309.7 1.6 fusion.7
  311.3 1.5 copy.42
  312.7 1.6 fusion.10
  314.3 1.5 copy.43
  315.8 1.6 fusion.13
  317.5 1.5 copy.44
  318.9 1.6 fusion.16
  320.6 1.5 copy.45
  322.1 1.6 fusion.19
  323.7 1.5 copy.46
  325.2 1.6 fusion.22
  326.8 1.5 copy.47
  328.4 2.5 constant_dynamic-update-slice_fusion.38
  330.9 2.4 constant_dynamic-update-slice_fusion.37
  333.2 2.4 constant_dynamic-update-slice_fusion.36
  335.6 2.4 constant_dynamic-update-slice_fusion.35
  341.5 11.4 %gather_fusion.1 = f32[1024,1536]{1,0:T(8,128)} fusion(f32[1536,1536]{1,0:T(8,128)} %constant_dynamic-update-slice_fusion.32, s32[1024]{0:T(1024)S(1)} %broadcast_clamp_fusion), kind=kCustom, calls=%fused_computation.1 | custom fusion | bytes 12587008 | tf_op jit(solution)/shard_map/jit(_take)/gather | solution.py:92
  352.9 5.9 broadcast_select_fusion
  362.8 209.9 %reduce-scatter.2.cloned.1.call-done = f32[8,1536]{1,0:T(8,128)} async-done(((f32[1024,1536]{1,0:T(8,128)}), f32[8,1536]{1,0:T(8,128)}) %reduce-scatter.2.cloned.1.call-update) | async-done | bytes 49168 | tf_op jit(solution)/shard_map/reduce_scatter | solution.py:94
  572.7 12.3 %all_gather.3 = f32[32,1536]{1,0:T(8,128)S(1)} all-gather(f32[8,1536]{1,0:T(8,128)} %reduce-scatter.2.cloned.1.call-done), channel_id=1, replica_groups=mesh['redist'=32,'rep'=4] {'rep'}, dimensions={0}, use_global_device_ids=true | all-gather | bytes 245760 | tf_op jit(solution)/shard_map/all_gather | solution.py:95
  585.5 1.7 dynamic_update_slice.8
  588.2 2.3 add.795
  (51 shorter events, 19.9 us)
Async XLA Ops:
  144.4 134.6 %copy-start.6 = (s32[1024]{0:T(1024)S(1)}, s32[1024]{0:T(1024)}, u32[]{:S(2)}) copy-start(s32[1024]{0:T(1024)} %param.7) | copy-start | bytes 12292
  144.4 153.9 %copy-start = (s32[128]{0:T(128)S(1)}, s32[128]{0:T(128)}, u32[]{:S(2)}) copy-start(s32[128]{0:T(128)} %param.6) | copy-start | bytes 1540
  250.3 50.5 %all-to-all-start = ((bf16[32,32,2,192]{3,1,2,0:T(8,128)(2,1)}), bf16[32,32,2,192]{3,1,2,0:T(8,128)(2,1)S(1)}, u32[]{:S(2)}, u32[]{:S(2)}) async-start(bf16[32,32,2,192]{3,1,2,0:T(8,128)(2,1)} %constant_dynamic-update-slice_fusion), calls=%async_computation | async-start | bytes 2097152 | tf_op jit(solution)/shard_map/all_to_all | solution.py:56
  258.8 313.9 %reduce-scatter.2.cloned.1.call-start = ((), (), s32[]{:S(2)}) async-start(), calls=%async_computation.2 | async-start | bytes 6340608 | tf_op jit(solution)/shard_map/reduce_scatter | solution.py:94
  305.7 10.1 %copy-start.5 = (s32[192,192]{1,0:T(8,128)S(1)}, s32[192,192]{1,0:T(8,128)}, u32[]{:S(2)}) copy-start(s32[192,192]{1,0:T(8,128)} %get-tuple-element.180) | copy-start | bytes 442372
  328.4 9.7 %copy-start.1 = (f32[192,1536]{1,0:T(8,128)S(1)}, f32[192,1536]{1,0:T(8,128)}, u32[]{:S(2)}) copy-start(f32[192,1536]{1,0:T(8,128)} %copy.45) | copy-start | bytes 3538948
  328.4 10.8 %copy-start.2 = (f32[192,1536]{1,0:T(8,128)S(1)}, f32[192,1536]{1,0:T(8,128)}, u32[]{:S(2)}) copy-start(f32[192,1536]{1,0:T(8,128)} %copy.46) | copy-start | bytes 3538948
  328.4 11.9 %copy-start.3 = (f32[192,1536]{1,0:T(8,128)S(1)}, f32[192,1536]{1,0:T(8,128)}, u32[]{:S(2)}) copy-start(f32[192,1536]{1,0:T(8,128)} %copy.47) | copy-start | bytes 3538948
  587.2 1.0 copy-start.4
Sparse Core Ops, SparseCore 0:
  359.0 213.6 reduce-scatter.1
